TPU v7x, 512 devices: a whole 4x8x8 slice. The times are simulated.
512 devices in a mesh: dp: 2 (over x_hi), blk: 32 (over z, x_lo, core), uly: 8 (over y).
Axes of the slice: x: 4 (x_hi: 2, x_lo: 2; x = x_hi * 2 + x_lo), y: 8, z: 8, core: 2. Of those that a mesh axis runs over, the one named last changes fastest.
Arguments:
- queries: bfloat16 [65536, 4096], P(('dp', 'blk', 'uly')), parts along dimension 0, may hold values from -24 to 24
- keys: bfloat16 [65536, 1024], P(('dp', 'blk', 'uly')), parts along dimension 0, may hold values from -12 to 12
- values: bfloat16 [65536, 1024], P(('dp', 'blk', 'uly')), parts along dimension 0, may hold values from -6 to 6
- doc_lengths: int32 [42], P('dp'), parts along dimension 0, may hold values from 1 to 2048, 32768 in all
Outputs:
- attended: bfloat16 [65536, 4096], P(('dp', 'blk', 'uly')), parts along dimension 0
There are 2 independent parts, one for each index of `dp`. A program takes and returns all parts, laid end to end along the dimension named above; each array names one. Nothing has to cross between parts.
Inputs may be any that keep to these rules, and one draw needn't show every extreme that they name: `doc_lengths`: the 21 lengths sum to 32768; the longest is exactly 2048.
All inputs are finite; a program needn't handle non-finite values.
Results may differ from a plain program's by a relative error of at most 0.0055.
Values may be sent and summed in bfloat16 or wider, within the bound.
No kernel may reach another device: no remote copies, remote signals or barrier semaphores. Data moves between devices by JAX's collectives and lax.ppermute only.
A program may use at most 64 MiB of HBM per device.

v0:
```python
import math

import jax
import jax.numpy as jnp
from jax import lax
from jax.sharding import PartitionSpec as P

QUERY_HEADS = 32
KEY_VALUE_HEADS = 8
HEAD_SIZE = 128
CYCLE = 2


NEG_FILL = -1e30


def passed_along(block, axis, distance):
    devices = range(lax.axis_size(axis))
    route = [(i - distance, i) for i in devices if i - distance in devices]
    return lax.ppermute(block, axis, route)


def doc_index(positions, doc_lengths):
    ends = jnp.cumsum(doc_lengths)
    return jnp.sum((positions[:, None] >= ends[None, :]).astype(jnp.int32), axis=1)


def per_device(queries, keys, values, doc_lengths):
    token_rows = queries.shape[0]
    q_heads = queries.reshape(token_rows, QUERY_HEADS, HEAD_SIZE)
    kv_heads = jnp.stack(
        [
            keys.reshape(token_rows, KEY_VALUE_HEADS, HEAD_SIZE),
            values.reshape(token_rows, KEY_VALUE_HEADS, HEAD_SIZE),
        ],
        axis=2,
    )
    q_local, kv_local = (
        lax.all_to_all(q_heads, "uly", split_axis=1, concat_axis=0, tiled=True),
        lax.all_to_all(kv_heads, "uly", split_axis=1, concat_axis=0, tiled=True),
    )
    block = q_local.shape[0]
    groups = kv_local.shape[1]
    group_repeat = QUERY_HEADS // KEY_VALUE_HEADS
    sub_rows = min(block, 512)
    pieces = block // sub_rows
    position = lax.axis_index("blk")
    rows = jnp.arange(block, dtype=jnp.int32)
    q_pos = position * block + rows
    q_doc = doc_index(q_pos, doc_lengths)
    q_parts = q_local.reshape(pieces, sub_rows, groups, group_repeat, HEAD_SIZE)
    pos_parts = q_pos.reshape(pieces, sub_rows)
    doc_parts = q_doc.reshape(pieces, sub_rows)
    scale = 1.0 / math.sqrt(HEAD_SIZE)

    def attend(state, kv_piece, back):
        k_pos = (position - back) * block + rows
        k_doc = doc_index(k_pos, doc_lengths)
        key_part = kv_piece[:, :, 0, :]
        value_part = kv_piece[:, :, 1, :]

        def one_part(items):
            q_part, pos_part, doc_part, peak, total, summed = items
            allowed = (
                (k_pos[None, :] <= pos_part[:, None])
                & (k_pos[None, :] >= 0)
                & (k_doc[None, :] == doc_part[:, None])
            )
            scores = (
                jnp.einsum("qgrd,kgd->qgrk", q_part, key_part, preferred_element_type=jnp.float32)
                * scale
            )
            scores = jnp.where(allowed[:, None, None, :], scores, NEG_FILL)
            new_peak = jnp.maximum(peak, jnp.max(scores, axis=-1))
            weights = jnp.where(
                allowed[:, None, None, :], jnp.exp(scores - new_peak[..., None]), 0.0
            )
            factor = jnp.exp(peak - new_peak)
            new_total = total * factor + jnp.sum(weights, axis=-1)
            update = jnp.einsum(
                "qgrk,kgd->qgrd",
                weights.astype(jnp.bfloat16),
                value_part,
                preferred_element_type=jnp.float32,
            )
            return (new_peak, new_total, summed * factor[..., None] + update)

        peak, total, summed = state
        return lax.map(one_part, (q_parts, pos_parts, doc_parts, peak, total, summed))

    start_state = (
        jnp.full((pieces, sub_rows, groups, group_repeat), NEG_FILL, jnp.float32),
        jnp.zeros((pieces, sub_rows, groups, group_repeat), jnp.float32),
        jnp.zeros((pieces, sub_rows, groups, group_repeat, HEAD_SIZE), jnp.float32),
    )
    state = attend(start_state, kv_local, 0)
    moving = kv_local
    for back in range(1, CYCLE + 1):
        moving = passed_along(moving, "blk", 1)
        state = attend(state, moving, back)
    peak, total, summed = state
    result = (
        (summed / total[..., None])
        .astype(jnp.bfloat16)
        .reshape(block, groups * group_repeat, HEAD_SIZE)
    )
    returned = lax.all_to_all(result, "uly", split_axis=0, concat_axis=1, tiled=True)
    return returned.reshape(token_rows, QUERY_HEADS * HEAD_SIZE)


def solution(mesh):
    in_specs = (
        P(("dp", "blk", "uly"), None),
        P(("dp", "blk", "uly"), None),
        P(("dp", "blk", "uly"), None),
        P("dp"),
    )
    out_specs = P(("dp", "blk", "uly"), None)
    return jax.shard_map(
        per_device, mesh=mesh, in_specs=in_specs, out_specs=out_specs, check_vma=False
    )
```

profile of v0, /device:TPU:7, one launch (start us, length us, event | category | flops | bytes accessed | tf_op | source)
XLA Modules:
  0.0 154.2 jit_solution(17214267690925940196)
XLA Ops:
  0.0 1.1 copy.74
  1.1 1.1 copy.75
  2.3 1.0 copy.76
  3.3 6.8 %all-to-all-start.1 = ((bf16[128,8,2,128]{3,0,2,1:T(8,128)(2,1)}), bf16[128,8,2,128]{3,0,2,1:T(8,128)(2,1)S(1)}, u32[]{:S(2)}, u32[]{:S(2)}) async-start(bf16[128,8,2,128]{3,0,2,1:T(8,128)(2,1)} %copy.76), calls=%async_computation.1 | async-start | bytes 1048576 | tf_op jit(solution)/shard_map/all_to_all | solution.py:40
  10.2 2.3 %copy.71 = bf16[128,4096]{0,1:T(8,128)(2,1)} copy(bf16[128,4096]{1,0:T(8,128)(2,1)} %param.10) | data formatting | bytes 2097152 | tf_op args[0]
  12.4 15.7 %all-to-all-done.1 = bf16[128,8,2,128]{3,0,2,1:T(8,128)(2,1)S(1)} async-done(((bf16[128,8,2,128]{3,0,2,1:T(8,128)(2,1)}), bf16[128,8,2,128]{3,0,2,1:T(8,128)(2,1)S(1)}, u32[]{:S(2)}, u32[]{:S(2)}) %all-to-all-start.1) | async-done | bytes 524320 | tf_op jit(solution)/shard_map/all_to_all | solution.py:40
  28.1 3.6 %all-to-all-start = ((bf16[128,32,128]{0,2,1:T(8,128)(2,1)}), bf16[128,32,128]{0,2,1:T(8,128)(2,1)S(1)}, u32[]{:S(2)}, u32[]{:S(2)}) async-start(bf16[128,32,128]{0,2,1:T(8,128)(2,1)} %bitcast.1), calls=%async_computation | async-start | bytes 2097152 | tf_op jit(solution)/shard_map/all_to_all | solution.py:39
  31.8 4.6 %collective-permute-start = (bf16[1024,1,2,128]{3,0,2,1:T(8,128)(2,1)S(1)}, bf16[1024,1,2,128]{3,0,2,1:T(8,128)(2,1)}, u32[]{:S(2)}, u32[]{:S(2)}) collective-permute-start(bf16[1024,1,2,128]{3,0,2,1:T(8,128)(2,1)S(1)} %bitcast.378), channel_id=1, source_target_pairs={{0,8},{8,16},{16,24},{24,32},{32,40},{40,48},{48,56},{56,64},{64,7... | collective-permute-start | bytes 1572872 | tf_op jit(solution)/shard_map/ppermute | solution.py:20
  36.9 5.6 %collective-permute-done = bf16[1024,1,2,128]{3,0,2,1:T(8,128)(2,1)} collective-permute-done((bf16[1024,1,2,128]{3,0,2,1:T(8,128)(2,1)S(1)}, bf16[1024,1,2,128]{3,0,2,1:T(8,128)(2,1)}, u32[]{:S(2)}, u32[]{:S(2)}) %collective-permute-start) | collective-permute-done | bytes 524320 | tf_op jit(solution)/shard_map/ppermute | solution.py:20
  42.5 5.4 %collective-permute-start.1 = (bf16[1024,1,2,128]{3,0,2,1:T(8,128)(2,1)}, bf16[1024,1,2,128]{3,0,2,1:T(8,128)(2,1)}, u32[]{:S(2)}, u32[]{:S(2)}) collective-permute-start(bf16[1024,1,2,128]{3,0,2,1:T(8,128)(2,1)} %collective-permute-done), channel_id=1, source_target_pairs={{0,8},{8,16},{16,24},{24,32},{32,40},{40,48},{48,56},{56,64},{64,7... | collective-permute-start | bytes 1572872 | tf_op jit(solution)/shard_map/ppermute | solution.py:20
  47.9 1.8 %slice_bitcast_fusion.2 = (bf16[1024,1,128]{2,0,1:T(8,128)(2,1)}, bf16[1024,1,128]{2,0,1:T(8,128)(2,1)S(1)}) fusion(bf16[1024,1,2,128]{3,0,2,1:T(8,128)(2,1)} %collective-permute-done), kind=kLoop, calls=%fused_computation.110 | loop fusion | bytes 1048576 | tf_op jit(solution)/shard_map/squeeze | solution.py:60
  49.7 11.2 %all-to-all-done = bf16[128,32,128]{0,2,1:T(8,128)(2,1)S(1)} async-done(((bf16[128,32,128]{0,2,1:T(8,128)(2,1)}), bf16[128,32,128]{0,2,1:T(8,128)(2,1)S(1)}, u32[]{:S(2)}, u32[]{:S(2)}) %all-to-all-start) | async-done | bytes 1048608 | tf_op jit(solution)/shard_map/all_to_all | solution.py:39
  60.8 0.7 copy.73
  61.6 1.5 broadcast.271.clone.1
  63.1 17.4 %while.43 = (s32[]{:T(128)}, f32[2,512,1,4]{1,3,2,0:T(4,128)S(1)}, f32[2,512,1,4]{1,3,2,0:T(4,128)S(1)}, f32[2,512,1,4,128]{4,1,3,2,0:T(8,128)}, s32[2,512]{1,0:...) while((s32[]{:T(128)}, f32[2,512,1,4]{1,3,2,0:T(4,128)S(1)}, ...), condition=%wide.region_5.6_spmd.clone, body=%wide.region_2.0_spmd.clone.sunk | while | flops 1103377408 | bytes 46262468 | solution.py:89
  63.1 0.6 compare_and_fusion.6
  63.7 1.9 %fusion.123 = (f32[512,4]{0,1:T(4,128)S(1)}, f32[512,4,1024]{2,0,1:T(8,128)S(1)}) fusion(pred[512,1024]{1,0:T(8,128)(4,1)S(1)} %compare_and_fusion.6, bf16[1024,1,128]{2,0,1:T(8,128)(2,1)S(1)} %get-tuple-element.943, bf16[2,512,1,4,128]{4,1,3,2,0:T(8,128)(2,1)S(1)} %get-tuple-element.942, s32[]{:T(128)} %get-tuple-element.923), kind=kOutput, calls=%fused_computation.5.clone.1 | convolution fusion | flops 543160320 | bytes 9707524 | tf_op jit(solution)/shard_map/while/body/eval_jaxpr/qgrd,kgd->qgrk/dot_general | solution.py:70
  65.7 3.1 %fusion.126 = f32[2,512,1,4,128]{4,1,3,2,0:T(8,128)S(1)} fusion(f32[2,512,1,4,128]{4,1,3,2,0:T(8,128)S(1)} %copy-done.1, s32[]{:T(128)} %get-tuple-element.923, f32[512,4,1024]{2,0,1:T(8,128)S(1)} %get-tuple-element.864, f32[512,4]{0,1:T(4,128)S(1)} %get-tuple-element.866, pred[512,1024]{1,0:T(8,128)(4,1)S(1)} %compare_and_fusion.6, ...), kind=kOutput, calls=%fused_computation.15.clone.1 | convolution fusion | flops 547618816 | bytes 10240004 | tf_op jit(solution)/shard_map/while/body/eval_jaxpr/qgrk,kgd->qgrd/dot_general | solution.py:80
  68.8 2.9 %fusion.124 = f32[512,4]{0,1:T(4,128)S(1)} fusion(f32[512,4,1024]{2,0,1:T(8,128)S(1)} %get-tuple-element.864, f32[512,4]{0,1:T(4,128)S(1)} %get-tuple-element.866, pred[512,1024]{1,0:T(8,128)(4,1)S(1)} %compare_and_fusion.6), kind=kLoop, calls=%fused_computation.7.clone.1 | loop fusion | flops 10483712 | bytes 8929280 | tf_op jit(solution)/shard_map/while/body/eval_jaxpr/reduce_sum | solution.py:79
  71.8 0.6 compare_and_fusion.6
  72.4 1.9 %fusion.123 = (f32[512,4]{0,1:T(4,128)S(1)}, f32[512,4,1024]{2,0,1:T(8,128)S(1)}) fusion(pred[512,1024]{1,0:T(8,128)(4,1)S(1)} %compare_and_fusion.6, bf16[1024,1,128]{2,0,1:T(8,128)(2,1)S(1)} %get-tuple-element.943, bf16[2,512,1,4,128]{4,1,3,2,0:T(8,128)(2,1)S(1)} %get-tuple-element.942, s32[]{:T(128)} %get-tuple-element.923), kind=kOutput, calls=%fused_computation.5.clone.1 | convolution fusion | flops 543160320 | bytes 9707524 | tf_op jit(solution)/shard_map/while/body/eval_jaxpr/qgrd,kgd->qgrk/dot_general | solution.py:70
  74.4 3.1 %fusion.126 = f32[2,512,1,4,128]{4,1,3,2,0:T(8,128)S(1)} fusion(f32[2,512,1,4,128]{4,1,3,2,0:T(8,128)S(1)} %copy-done.1, s32[]{:T(128)} %get-tuple-element.923, f32[512,4,1024]{2,0,1:T(8,128)S(1)} %get-tuple-element.864, f32[512,4]{0,1:T(4,128)S(1)} %get-tuple-element.866, pred[512,1024]{1,0:T(8,128)(4,1)S(1)} %compare_and_fusion.6, ...), kind=kOutput, calls=%fused_computation.15.clone.1 | convolution fusion | flops 547618816 | bytes 10240004 | tf_op jit(solution)/shard_map/while/body/eval_jaxpr/qgrk,kgd->qgrd/dot_general | solution.py:80
  77.5 2.9 %fusion.124 = f32[512,4]{0,1:T(4,128)S(1)} fusion(f32[512,4,1024]{2,0,1:T(8,128)S(1)} %get-tuple-element.864, f32[512,4]{0,1:T(4,128)S(1)} %get-tuple-element.866, pred[512,1024]{1,0:T(8,128)(4,1)S(1)} %compare_and_fusion.6), kind=kLoop, calls=%fused_computation.7.clone.1 | loop fusion | flops 10483712 | bytes 8929280 | tf_op jit(solution)/shard_map/while/body/eval_jaxpr/reduce_sum | solution.py:79
  80.5 1.5 broadcast.271
  82.0 17.7 %while.44 = (s32[]{:T(128)}, f32[2,512,1,4]{1,3,2,0:T(4,128)S(1)}, f32[2,512,1,4]{1,3,2,0:T(4,128)S(1)}, f32[2,512,1,4,128]{4,1,3,2,0:T(8,128)}, f32[2,512,1,4]{...) while((s32[]{:T(128)}, f32[2,512,1,4]{1,3,2,0:T(4,128)S(1)}, ...), condition=%wide.region_10.11_spmd.clone, body=%wide.region_7.10_spmd.clone.sunk | while | flops 1103637504 | bytes 56772888 | solution.py:89
  82.0 0.6 compare_and_fusion.7
  82.7 1.9 %fusion.129 = (f32[512,4]{0,1:T(4,128)S(1)}, f32[512,4,1024]{2,0,1:T(8,128)S(1)}) fusion(pred[512,1024]{1,0:T(8,128)(4,1)S(1)} %compare_and_fusion.7, bf16[1024,1,128]{2,0,1:T(8,128)(2,1)S(1)} %get-tuple-element.986, bf16[2,512,1,4,128]{4,1,3,2,0:T(8,128)(2,1)S(1)} %get-tuple-element.985, s32[]{:T(128)} %get-tuple-element.962), kind=kOutput, calls=%fused_computation.39.clone.1 | convolution fusion | flops 543160320 | bytes 9707524 | tf_op jit(solution)/shard_map/while/body/eval_jaxpr/qgrd,kgd->qgrk/dot_general | solution.py:70
  84.6 3.1 %fusion.133 = f32[2,512,1,4,128]{4,1,3,2,0:T(8,128)S(1)} fusion(f32[2,512,1,4,128]{4,1,3,2,0:T(8,128)S(1)} %copy-done.4, s32[]{:T(128)} %get-tuple-element.962, f32[512,4,1024]{2,0,1:T(8,128)S(1)} %get-tuple-element.886, f32[512,4]{0,1:T(4,128)S(1)} %get-tuple-element.888, pred[512,1024]{1,0:T(8,128)(4,1)S(1)} %compare_and_fusion.7, ...), kind=kOutput, calls=%fused_computation.49.clone.1 | convolution fusion | flops 547880960 | bytes 11288580 | tf_op jit(solution)/shard_map/while/body/eval_jaxpr/qgrk,kgd->qgrd/dot_general | solution.py:80
  87.7 3.0 %fusion.131 = f32[512,4]{0,1:T(4,128)S(1)} fusion(f32[512,4,1024]{2,0,1:T(8,128)S(1)} %get-tuple-element.886, f32[512,4]{0,1:T(4,128)S(1)} %get-tuple-element.888, pred[512,1024]{1,0:T(8,128)(4,1)S(1)} %compare_and_fusion.7), kind=kLoop, calls=%fused_computation.41.clone.1 | loop fusion | flops 10483712 | bytes 8929280 | tf_op jit(solution)/shard_map/while/body/eval_jaxpr/reduce_sum | solution.py:79
  90.9 0.6 compare_and_fusion.7
  91.5 1.9 %fusion.129 = (f32[512,4]{0,1:T(4,128)S(1)}, f32[512,4,1024]{2,0,1:T(8,128)S(1)}) fusion(pred[512,1024]{1,0:T(8,128)(4,1)S(1)} %compare_and_fusion.7, bf16[1024,1,128]{2,0,1:T(8,128)(2,1)S(1)} %get-tuple-element.986, bf16[2,512,1,4,128]{4,1,3,2,0:T(8,128)(2,1)S(1)} %get-tuple-element.985, s32[]{:T(128)} %get-tuple-element.962), kind=kOutput, calls=%fused_computation.39.clone.1 | convolution fusion | flops 543160320 | bytes 9707524 | tf_op jit(solution)/shard_map/while/body/eval_jaxpr/qgrd,kgd->qgrk/dot_general | solution.py:70
  93.4 3.1 %fusion.133 = f32[2,512,1,4,128]{4,1,3,2,0:T(8,128)S(1)} fusion(f32[2,512,1,4,128]{4,1,3,2,0:T(8,128)S(1)} %copy-done.4, s32[]{:T(128)} %get-tuple-element.962, f32[512,4,1024]{2,0,1:T(8,128)S(1)} %get-tuple-element.886, f32[512,4]{0,1:T(4,128)S(1)} %get-tuple-element.888, pred[512,1024]{1,0:T(8,128)(4,1)S(1)} %compare_and_fusion.7, ...), kind=kOutput, calls=%fused_computation.49.clone.1 | convolution fusion | flops 547880960 | bytes 11288580 | tf_op jit(solution)/shard_map/while/body/eval_jaxpr/qgrk,kgd->qgrd/dot_general | solution.py:80
  96.6 3.0 %fusion.131 = f32[512,4]{0,1:T(4,128)S(1)} fusion(f32[512,4,1024]{2,0,1:T(8,128)S(1)} %get-tuple-element.886, f32[512,4]{0,1:T(4,128)S(1)} %get-tuple-element.888, pred[512,1024]{1,0:T(8,128)(4,1)S(1)} %compare_and_fusion.7), kind=kLoop, calls=%fused_computation.41.clone.1 | loop fusion | flops 10483712 | bytes 8929280 | tf_op jit(solution)/shard_map/while/body/eval_jaxpr/reduce_sum | solution.py:79
  99.7 1.8 %slice_bitcast_fusion = (bf16[1024,1,128]{2,0,1:T(8,128)(2,1)}, bf16[1024,1,128]{2,0,1:T(8,128)(2,1)S(1)}) fusion(bf16[1024,1,2,128]{3,0,2,1:T(8,128)(2,1)} %collective-permute-done.1), kind=kLoop, calls=%fused_computation.108 | loop fusion | bytes 1048576 | tf_op jit(solution)/shard_map/squeeze | solution.py:60
  101.4 17.6 %while.45 = (s32[]{:T(128)}, f32[2,512,1,4]{1,3,2,0:T(4,128)S(1)}, f32[2,512,1,4,128]{4,1,0,3,2:T(8,128)S(1)}, f32[2,512,1,4]{1,3,2,0:T(4,128)S(1)}, f32[2,512,1...) while((s32[]{:T(128)}, f32[2,512,1,4]{1,3,2,0:T(4,128)S(1)}, ...), condition=%wide.region_15.16_spmd.clone, body=%wide.region_12.15_spmd.clone.sunk | while | flops 1103637504 | bytes 39987416 | solution.py:89
  101.5 0.6 compare_and_fusion.8
  102.1 1.9 %fusion.136 = (f32[512,4]{0,1:T(4,128)S(1)}, f32[512,4,1024]{2,0,1:T(8,128)S(1)}) fusion(pred[512,1024]{1,0:T(8,128)(4,1)S(1)} %compare_and_fusion.8, bf16[1024,1,128]{2,0,1:T(8,128)(2,1)S(1)} %get-tuple-element.1029, bf16[2,512,1,4,128]{4,1,3,2,0:T(8,128)(2,1)S(1)} %get-tuple-element.1028, s32[]{:T(128)} %get-tuple-element.1006), kind=kOutput, calls=%fused_computation.73.clone.1 | convolution fusion | flops 543160320 | bytes 9707524 | tf_op jit(solution)/shard_map/while/body/eval_jaxpr/qgrd,kgd->qgrk/dot_general | solution.py:70
  104.0 3.1 %fusion.140 = f32[2,512,1,4,128]{4,1,0,3,2:T(8,128)S(1)} fusion(f32[2,512,1,4,128]{4,1,0,3,2:T(8,128)S(1)} %get-tuple-element.1008, s32[]{:T(128)} %get-tuple-element.1006, f32[512,4,1024]{2,0,1:T(8,128)S(1)} %get-tuple-element.907, f32[512,4]{0,1:T(4,128)S(1)} %get-tuple-element.909, pred[512,1024]{1,0:T(8,128)(4,1)S(1)} %compare_and_fusion.8, ...), kind=kOutput, calls=%fused_computation.83.clone.1 | convolution fusion | flops 547880960 | bytes 11288580 | tf_op jit(solution)/shard_map/while/body/eval_jaxpr/qgrk,kgd->qgrd/dot_general | solution.py:80
  107.1 3.0 %fusion.138 = f32[512,4]{0,1:T(4,128)S(1)} fusion(f32[512,4,1024]{2,0,1:T(8,128)S(1)} %get-tuple-element.907, f32[512,4]{0,1:T(4,128)S(1)} %get-tuple-element.909, pred[512,1024]{1,0:T(8,128)(4,1)S(1)} %compare_and_fusion.8), kind=kLoop, calls=%fused_computation.75.clone.1 | loop fusion | flops 10483712 | bytes 8929280 | tf_op jit(solution)/shard_map/while/body/eval_jaxpr/reduce_sum | solution.py:79
  110.3 0.6 compare_and_fusion.8
  110.9 1.9 %fusion.136 = (f32[512,4]{0,1:T(4,128)S(1)}, f32[512,4,1024]{2,0,1:T(8,128)S(1)}) fusion(pred[512,1024]{1,0:T(8,128)(4,1)S(1)} %compare_and_fusion.8, bf16[1024,1,128]{2,0,1:T(8,128)(2,1)S(1)} %get-tuple-element.1029, bf16[2,512,1,4,128]{4,1,3,2,0:T(8,128)(2,1)S(1)} %get-tuple-element.1028, s32[]{:T(128)} %get-tuple-element.1006), kind=kOutput, calls=%fused_computation.73.clone.1 | convolution fusion | flops 543160320 | bytes 9707524 | tf_op jit(solution)/shard_map/while/body/eval_jaxpr/qgrd,kgd->qgrk/dot_general | solution.py:70
  112.9 3.1 %fusion.140 = f32[2,512,1,4,128]{4,1,0,3,2:T(8,128)S(1)} fusion(f32[2,512,1,4,128]{4,1,0,3,2:T(8,128)S(1)} %get-tuple-element.1008, s32[]{:T(128)} %get-tuple-element.1006, f32[512,4,1024]{2,0,1:T(8,128)S(1)} %get-tuple-element.907, f32[512,4]{0,1:T(4,128)S(1)} %get-tuple-element.909, pred[512,1024]{1,0:T(8,128)(4,1)S(1)} %compare_and_fusion.8, ...), kind=kOutput, calls=%fused_computation.83.clone.1 | convolution fusion | flops 547880960 | bytes 11288580 | tf_op jit(solution)/shard_map/while/body/eval_jaxpr/qgrk,kgd->qgrd/dot_general | solution.py:80
  116.0 3.0 %fusion.138 = f32[512,4]{0,1:T(4,128)S(1)} fusion(f32[512,4,1024]{2,0,1:T(8,128)S(1)} %get-tuple-element.907, f32[512,4]{0,1:T(4,128)S(1)} %get-tuple-element.909, pred[512,1024]{1,0:T(8,128)(4,1)S(1)} %compare_and_fusion.8), kind=kLoop, calls=%fused_computation.75.clone.1 | loop fusion | flops 10483712 | bytes 8929280 | tf_op jit(solution)/shard_map/while/body/eval_jaxpr/reduce_sum | solution.py:79
  119.0 0.7 divide_convert_fusion
  119.8 0.8 copy.83
  120.6 31.5 %all_to_all.48 = bf16[1024,4,128]{2,1,0:T(4,128)(2,1)S(1)} all-to-all(bf16[1024,4,128]{2,1,0:T(4,128)(2,1)S(1)} %copy.83), channel_id=1, replica_groups=mesh['dp'=2,'blk'=32,'uly'=8] {'uly'}, dimensions={0} | all-to-all | bytes 2097152 | tf_op jit(solution)/shard_map/all_to_all | solution.py:107
  152.2 0.7 copy.85
  152.9 1.3 copy.86
  (87 shorter events, 1.2 us)
Async XLA Ops:
  0.0 36.4 %copy-start.9 = (s32[21]{0:T(128)S(1)}, s32[21]{0:T(128)}, u32[]{:S(2)}) copy-start(s32[21]{0:T(128)} %param.13) | copy-start | bytes 256
  3.3 24.8 %all-to-all-start.1 = ((bf16[128,8,2,128]{3,0,2,1:T(8,128)(2,1)}), bf16[128,8,2,128]{3,0,2,1:T(8,128)(2,1)S(1)}, u32[]{:S(2)}, u32[]{:S(2)}) async-start(bf16[128,8,2,128]{3,0,2,1:T(8,128)(2,1)} %copy.76), calls=%async_computation.1 | async-start | bytes 1048576 | tf_op jit(solution)/shard_map/all_to_all | solution.py:40
  28.1 32.7 %all-to-all-start = ((bf16[128,32,128]{0,2,1:T(8,128)(2,1)}), bf16[128,32,128]{0,2,1:T(8,128)(2,1)S(1)}, u32[]{:S(2)}, u32[]{:S(2)}) async-start(bf16[128,32,128]{0,2,1:T(8,128)(2,1)} %bitcast.1), calls=%async_computation | async-start | bytes 2097152 | tf_op jit(solution)/shard_map/all_to_all | solution.py:39
  31.8 10.8 %collective-permute-start = (bf16[1024,1,2,128]{3,0,2,1:T(8,128)(2,1)S(1)}, bf16[1024,1,2,128]{3,0,2,1:T(8,128)(2,1)}, u32[]{:S(2)}, u32[]{:S(2)}) collective-permute-start(bf16[1024,1,2,128]{3,0,2,1:T(8,128)(2,1)S(1)} %bitcast.378), channel_id=1, source_target_pairs={{0,8},{8,16},{16,24},{24,32},{32,40},{40,48},{48,56},{56,64},{64,7... | collective-permute-start | bytes 1572872 | tf_op jit(solution)/shard_map/ppermute | solution.py:20
  42.5 57.1 %collective-permute-start.1 = (bf16[1024,1,2,128]{3,0,2,1:T(8,128)(2,1)}, bf16[1024,1,2,128]{3,0,2,1:T(8,128)(2,1)}, u32[]{:S(2)}, u32[]{:S(2)}) collective-permute-start(bf16[1024,1,2,128]{3,0,2,1:T(8,128)(2,1)} %collective-permute-done), channel_id=1, source_target_pairs={{0,8},{8,16},{16,24},{24,32},{32,40},{40,48},{48,56},{56,64},{64,7... | collective-permute-start | bytes 1572872 | tf_op jit(solution)/shard_map/ppermute | solution.py:20
  63.1 2.6 %copy-start.1 = (f32[2,512,1,4,128]{4,1,3,2,0:T(8,128)S(1)}, f32[2,512,1,4,128]{4,1,3,2,0:T(8,128)}, u32[]{:S(2)}) copy-start(f32[2,512,1,4,128]{4,1,3,2,0:T(8,128)} %get-tuple-element.926) | copy-start | bytes 6291460 | tf_op jit(solution)/shard_map/while
  68.8 2.9 %copy-start.2 = (f32[2,512,1,4,128]{4,1,3,2,0:T(8,128)}, f32[2,512,1,4,128]{4,1,3,2,0:T(8,128)S(1)}, u32[]{:S(2)}) copy-start(f32[2,512,1,4,128]{4,1,3,2,0:T(8,128)S(1)} %fusion.126) | copy-start | bytes 6291460 | tf_op jit(solution)/shard_map/while
  71.8 2.6 %copy-start.1 = (f32[2,512,1,4,128]{4,1,3,2,0:T(8,128)S(1)}, f32[2,512,1,4,128]{4,1,3,2,0:T(8,128)}, u32[]{:S(2)}) copy-start(f32[2,512,1,4,128]{4,1,3,2,0:T(8,128)} %get-tuple-element.926) | copy-start | bytes 6291460 | tf_op jit(solution)/shard_map/while
  77.5 2.9 %copy-start.2 = (f32[2,512,1,4,128]{4,1,3,2,0:T(8,128)}, f32[2,512,1,4,128]{4,1,3,2,0:T(8,128)S(1)}, u32[]{:S(2)}) copy-start(f32[2,512,1,4,128]{4,1,3,2,0:T(8,128)S(1)} %fusion.126) | copy-start | bytes 6291460 | tf_op jit(solution)/shard_map/while
  81.9 19.5 %copy-start = (f32[2,512,1,4,128]{4,1,0,3,2:T(8,128)S(1)}, f32[2,512,1,4,128]{4,1,0,3,2:T(8,128)}, u32[]{:S(2)}) copy-start(f32[2,512,1,4,128]{4,1,0,3,2:T(8,128)} %custom-call) | copy-start | bytes 6291460
  82.0 2.6 %copy-start.3 = (f32[2,512,1,4,128]{4,1,3,2,0:T(8,128)S(1)}, f32[2,512,1,4,128]{4,1,3,2,0:T(8,128)}, u32[]{:S(2)}) copy-start(f32[2,512,1,4,128]{4,1,3,2,0:T(8,128)} %get-tuple-element.988) | copy-start | bytes 6291460 | tf_op jit(solution)/shard_map/while
  82.0 2.6 %copy-start.4 = (f32[2,512,1,4,128]{4,1,3,2,0:T(8,128)S(1)}, f32[2,512,1,4,128]{4,1,3,2,0:T(8,128)}, u32[]{:S(2)}) copy-start(f32[2,512,1,4,128]{4,1,3,2,0:T(8,128)} %get-tuple-element.965) | copy-start | bytes 6291460 | tf_op jit(solution)/shard_map/while
  82.0 2.6 %copy-start.7 = (bf16[1024,1,128]{2,0,1:T(8,128)(2,1)S(1)}, bf16[1024,1,128]{2,0,1:T(8,128)(2,1)}, u32[]{:S(2)}) copy-start(bf16[1024,1,128]{2,0,1:T(8,128)(2,1)} %get-tuple-element.989) | copy-start | bytes 786436 | tf_op jit(solution)/shard_map/while
  87.7 3.1 %copy-start.5 = (f32[2,512,1,4,128]{4,1,3,2,0:T(8,128)}, f32[2,512,1,4,128]{4,1,3,2,0:T(8,128)S(1)}, u32[]{:S(2)}) copy-start(f32[2,512,1,4,128]{4,1,3,2,0:T(8,128)S(1)} %fusion.133) | copy-start | bytes 6291460 | tf_op jit(solution)/shard_map/while
  90.8 2.6 %copy-start.3 = (f32[2,512,1,4,128]{4,1,3,2,0:T(8,128)S(1)}, f32[2,512,1,4,128]{4,1,3,2,0:T(8,128)}, u32[]{:S(2)}) copy-start(f32[2,512,1,4,128]{4,1,3,2,0:T(8,128)} %get-tuple-element.988) | copy-start | bytes 6291460 | tf_op jit(solution)/shard_map/while
  90.8 2.6 %copy-start.4 = (f32[2,512,1,4,128]{4,1,3,2,0:T(8,128)S(1)}, f32[2,512,1,4,128]{4,1,3,2,0:T(8,128)}, u32[]{:S(2)}) copy-start(f32[2,512,1,4,128]{4,1,3,2,0:T(8,128)} %get-tuple-element.965) | copy-start | bytes 6291460 | tf_op jit(solution)/shard_map/while
  90.8 2.6 %copy-start.7 = (bf16[1024,1,128]{2,0,1:T(8,128)(2,1)S(1)}, bf16[1024,1,128]{2,0,1:T(8,128)(2,1)}, u32[]{:S(2)}) copy-start(bf16[1024,1,128]{2,0,1:T(8,128)(2,1)} %get-tuple-element.989) | copy-start | bytes 786436 | tf_op jit(solution)/shard_map/while
  96.5 3.1 %copy-start.5 = (f32[2,512,1,4,128]{4,1,3,2,0:T(8,128)}, f32[2,512,1,4,128]{4,1,3,2,0:T(8,128)S(1)}, u32[]{:S(2)}) copy-start(f32[2,512,1,4,128]{4,1,3,2,0:T(8,128)S(1)} %fusion.133) | copy-start | bytes 6291460 | tf_op jit(solution)/shard_map/while
  101.4 2.6 %copy-start.6 = (f32[2,512,1,4,128]{4,1,3,2,0:T(8,128)S(1)}, f32[2,512,1,4,128]{4,1,3,2,0:T(8,128)}, u32[]{:S(2)}) copy-start(f32[2,512,1,4,128]{4,1,3,2,0:T(8,128)} %get-tuple-element.1030) | copy-start | bytes 6291460 | tf_op jit(solution)/shard_map/while
  101.4 2.6 %copy-start.8 = (bf16[1024,1,128]{2,0,1:T(8,128)(2,1)S(1)}, bf16[1024,1,128]{2,0,1:T(8,128)(2,1)}, u32[]{:S(2)}) copy-start(bf16[1024,1,128]{2,0,1:T(8,128)(2,1)} %get-tuple-element.1031) | copy-start | bytes 786436 | tf_op jit(solution)/shard_map/while
  110.2 2.6 %copy-start.6 = (f32[2,512,1,4,128]{4,1,3,2,0:T(8,128)S(1)}, f32[2,512,1,4,128]{4,1,3,2,0:T(8,128)}, u32[]{:S(2)}) copy-start(f32[2,512,1,4,128]{4,1,3,2,0:T(8,128)} %get-tuple-element.1030) | copy-start | bytes 6291460 | tf_op jit(solution)/shard_map/while
  110.2 2.6 %copy-start.8 = (bf16[1024,1,128]{2,0,1:T(8,128)(2,1)S(1)}, bf16[1024,1,128]{2,0,1:T(8,128)(2,1)}, u32[]{:S(2)}) copy-start(bf16[1024,1,128]{2,0,1:T(8,128)(2,1)} %get-tuple-element.1031) | copy-start | bytes 786436 | tf_op jit(solution)/shard_map/while
where the time goes:
time: 155 us; the launch traced here: 154 us
  waiting for transfers between devices  32.5 us (21%)
  blocking collectives  31.5 us (20%)
  matrix products  29.9 us (19%)
  other arithmetic  23.1 us (15%)
  starting transfers between devices  20.4 us (13%)
  local copies, waits for them, and re-layouts  16 us (10%)
    all_to_all x1, blocking collectives, per_device(): lax.all_to_all(result, 'uly', split_axis=0, concat_axis=1, tiled=True)  31.5 us
    dot_general x6, matrix products, one_part(): jnp.einsum('qgrk,kgd->qgrd', weights.astype(jnp.bfloat16), value_part, pr...  18.5 us
    reduce_sum x6, other arithmetic, one_part(): new_total = total * factor + jnp.sum(weights, axis=-1)  18 us
    all_to_all x1, waiting for transfers between devices, per_device(): lax.all_to_all(kv_heads, 'uly', split_axis=1, concat_axis=0, tiled=True)  15.7 us
    dot_general x6, matrix products, one_part(): jnp.einsum('qgrd,kgd->qgrk', q_part, key_part, preferred_element_type=jnp...  11.4 us
    all_to_all x1, waiting for transfers between devices, per_device(): lax.all_to_all(q_heads, 'uly', split_axis=1, concat_axis=0, tiled=True)  11.2 us
    ppermute x2, starting transfers between devices, passed_along(): return lax.ppermute(block, axis, route)  10 us
    all_to_all x1, starting transfers between devices, per_device(): lax.all_to_all(kv_heads, 'uly', split_axis=1, concat_axis=0, tiled=True)  6.82 us
  transfers between devices with their start and end apart: 4, of which 3 were waited for; matrix products, arithmetic and copies ran while one was open for 28% of the time, Pallas kernels for 0%

commit v1 on v0

v1 whole, which is shorter than its diff:
```python
import functools
import math

import jax
import jax.numpy as jnp
from jax import lax
from jax.experimental import pallas as pl
from jax.experimental.pallas import tpu as pltpu
from jax.sharding import PartitionSpec as P

QUERY_HEADS = 32
KEY_VALUE_HEADS = 8
HEAD_SIZE = 128
CYCLE = 2

Q_TILE = 256
K_TILE = 256

NEG_FILL = -1e30


def passed_along(block, axis, distance):
    devices = range(lax.axis_size(axis))
    route = [(i - distance, i) for i in devices if i - distance in devices]
    return lax.ppermute(block, axis, route)


def doc_index(positions, doc_lengths):
    ends = jnp.cumsum(doc_lengths)
    return jnp.sum((positions[:, None] >= ends[None, :]).astype(jnp.int32), axis=1)


def attend_kernel(bounds_ref, q_doc_ref, k_doc_ref, q_ref, k_ref, v_ref, o_ref,
                  peak_sc, total_sc, summed_sc, *, heads, ext_off):
    i = pl.program_id(0)
    lo = bounds_ref[2 * i]
    hi = bounds_ref[2 * i + 1]
    peak_sc[...] = jnp.full(peak_sc.shape, NEG_FILL, jnp.float32)
    total_sc[...] = jnp.zeros(total_sc.shape, jnp.float32)
    summed_sc[...] = jnp.zeros(summed_sc.shape, jnp.float32)
    q_doc = q_doc_ref[...]
    q_col = i * Q_TILE + ext_off + lax.broadcasted_iota(jnp.int32, (Q_TILE, 1), 0)
    scale = 1.0 / math.sqrt(HEAD_SIZE)

    def body(j, carry):
        start = pl.multiple_of(j * K_TILE, K_TILE)
        k = k_ref[pl.ds(start, K_TILE), :]
        v = v_ref[pl.ds(start, K_TILE), :]
        k_doc = k_doc_ref[pl.ds(j, 1), :]
        k_col = start + lax.broadcasted_iota(jnp.int32, (1, K_TILE), 1)
        allowed = (k_doc == q_doc) & (k_col <= q_col)
        for h in range(heads):
            q = q_ref[:, h * HEAD_SIZE:(h + 1) * HEAD_SIZE]
            scores = lax.dot_general(
                q, k, (((1,), (1,)), ((), ())), preferred_element_type=jnp.float32
            ) * scale
            scores = jnp.where(allowed, scores, NEG_FILL)
            peak = peak_sc[h]
            new_peak = jnp.maximum(peak, jnp.max(scores, axis=1, keepdims=True))
            weights = jnp.where(allowed, jnp.exp(scores - new_peak), 0.0)
            factor = jnp.exp(peak - new_peak)
            total_sc[h] = total_sc[h] * factor + jnp.sum(weights, axis=1, keepdims=True)
            summed_sc[h] = summed_sc[h] * factor + jnp.dot(
                weights.astype(jnp.bfloat16), v, preferred_element_type=jnp.float32
            )
            peak_sc[h] = new_peak
        return carry

    lax.fori_loop(lo, hi + 1, body, 0)
    for h in range(heads):
        o_ref[:, h * HEAD_SIZE:(h + 1) * HEAD_SIZE] = (
            summed_sc[h] / total_sc[h]
        ).astype(o_ref.dtype)


def attend(bounds, q_doc, k_doc, q2, k_ext, v_ext, heads, ext_off):
    rows = q2.shape[0]
    ext = k_ext.shape[0]
    n_q = rows // Q_TILE
    n_k = ext // K_TILE
    kernel = functools.partial(attend_kernel, heads=heads, ext_off=ext_off)
    grid_spec = pltpu.PrefetchScalarGridSpec(
        num_scalar_prefetch=1,
        grid=(n_q,),
        in_specs=[
            pl.BlockSpec((Q_TILE, 1), lambda i, b: (i, 0)),
            pl.BlockSpec((n_k, K_TILE), lambda i, b: (0, 0)),
            pl.BlockSpec((Q_TILE, heads * HEAD_SIZE), lambda i, b: (i, 0)),
            pl.BlockSpec((ext, HEAD_SIZE), lambda i, b: (0, 0)),
            pl.BlockSpec((ext, HEAD_SIZE), lambda i, b: (0, 0)),
        ],
        out_specs=pl.BlockSpec((Q_TILE, heads * HEAD_SIZE), lambda i, b: (i, 0)),
        scratch_shapes=[
            pltpu.VMEM((heads, Q_TILE, 1), jnp.float32),
            pltpu.VMEM((heads, Q_TILE, 1), jnp.float32),
            pltpu.VMEM((heads, Q_TILE, HEAD_SIZE), jnp.float32),
        ],
    )
    return pl.pallas_call(
        kernel,
        grid_spec=grid_spec,
        out_shape=jax.ShapeDtypeStruct((rows, heads * HEAD_SIZE), jnp.bfloat16),
    )(bounds, q_doc, k_doc, q2, k_ext, v_ext)


def tile_bounds(position, block, ext_off, ext, doc_lengths):
    ends = jnp.cumsum(doc_lengths)
    starts = ends - doc_lengths
    n_q = block // Q_TILE
    n_k = ext // K_TILE
    first = position * block + jnp.arange(n_q, dtype=jnp.int32) * Q_TILE
    first_doc = jnp.clip(doc_index(first, doc_lengths), 0, doc_lengths.shape[0] - 1)
    lo_key = starts[first_doc] - position * block + ext_off
    lo_key = jnp.maximum(lo_key, 0)
    hi_key = jnp.arange(n_q, dtype=jnp.int32) * Q_TILE + Q_TILE - 1 + ext_off
    hi = jnp.clip(hi_key // K_TILE, 0, n_k - 1)
    lo = jnp.clip(lo_key // K_TILE, 0, hi)
    return jnp.stack([lo, hi], axis=1).reshape(-1).astype(jnp.int32)


def per_device(queries, keys, values, doc_lengths):
    token_rows = queries.shape[0]
    q_heads = queries.reshape(token_rows, QUERY_HEADS, HEAD_SIZE)
    kv_heads = jnp.stack(
        [
            keys.reshape(token_rows, KEY_VALUE_HEADS, HEAD_SIZE),
            values.reshape(token_rows, KEY_VALUE_HEADS, HEAD_SIZE),
        ],
        axis=2,
    )
    q_local, kv_local = (
        lax.all_to_all(q_heads, "uly", split_axis=1, concat_axis=0, tiled=True),
        lax.all_to_all(kv_heads, "uly", split_axis=1, concat_axis=0, tiled=True),
    )
    block = q_local.shape[0]
    heads = q_local.shape[1]
    ext_off = CYCLE * block
    ext = ext_off + block
    position = lax.axis_index("blk")

    pieces = [kv_local]
    moving = kv_local
    for back in range(1, CYCLE + 1):
        moving = passed_along(moving, "blk", 1)
        pieces.append(moving)
    kv_ext = jnp.concatenate(pieces[::-1], axis=0)
    k_ext = kv_ext[:, 0, 0, :]
    v_ext = kv_ext[:, 0, 1, :]

    q_pos = position * block + jnp.arange(block, dtype=jnp.int32)
    q_doc = doc_index(q_pos, doc_lengths).reshape(block, 1)
    k_pos = position * block - ext_off + jnp.arange(ext, dtype=jnp.int32)
    k_doc = jnp.where(k_pos >= 0, doc_index(k_pos, doc_lengths), -1)
    k_doc = k_doc.reshape(ext // K_TILE, K_TILE)
    bounds = tile_bounds(position, block, ext_off, ext, doc_lengths)

    q2 = q_local.reshape(block, heads * HEAD_SIZE)
    result = attend(bounds, q_doc, k_doc, q2, k_ext, v_ext, heads, ext_off)
    result = result.reshape(block, heads, HEAD_SIZE)
    returned = lax.all_to_all(result, "uly", split_axis=0, concat_axis=1, tiled=True)
    return returned.reshape(token_rows, QUERY_HEADS * HEAD_SIZE)


def solution(mesh):
    in_specs = (
        P(("dp", "blk", "uly"), None),
        P(("dp", "blk", "uly"), None),
        P(("dp", "blk", "uly"), None),
        P("dp"),
    )
    out_specs = P(("dp", "blk", "uly"), None)
    return jax.shard_map(
        per_device, mesh=mesh, in_specs=in_specs, out_specs=out_specs, check_vma=False
    )
```

time: 155 us -> 165 us (1.065)
  the two profiles are of different devices: /device:TPU:7 before, /device:TPU:70 now
where the time goes in v1:
time: 165 us; the launch traced here: 164 us
  Pallas kernels  74.8 us (45%)
  waiting for transfers between devices  37.4 us (23%)
  blocking collectives  21.3 us (13%)
  starting transfers between devices  14.8 us (9%)
  local copies, waits for them, and re-layouts  13.5 us (8%)
  other arithmetic  2.41 us (1%)
    pallas_call x1, Pallas kernels, attend(): pl.pallas_call(kernel, grid_spec=grid_spec, out_shape=jax.ShapeDtypeStruc...  74.8 us
    all_to_all x1, blocking collectives, per_device(): lax.all_to_all(result, 'uly', split_axis=0, concat_axis=1, tiled=True)  21.3 us
    all_to_all x1, waiting for transfers between devices, per_device(): lax.all_to_all(kv_heads, 'uly', split_axis=1, concat_axis=0, tiled=True)  16.2 us
    all_to_all x1, waiting for transfers between devices, per_device(): lax.all_to_all(q_heads, 'uly', split_axis=1, concat_axis=0, tiled=True)  14 us
    ppermute x2, waiting for transfers between devices, passed_along(): return lax.ppermute(block, axis, route)  7.17 us
    all_to_all x1, starting transfers between devices, per_device(): lax.all_to_all(kv_heads, 'uly', split_axis=1, concat_axis=0, tiled=True)  7.1 us
    unnamed x8, local copies, waits for them, and re-layouts  4.71 us
    ppermute x2, starting transfers between devices, passed_along(): return lax.ppermute(block, axis, route)  4.09 us
  transfers between devices with their start and end apart: 4, of which 3 were waited for; matrix products, arithmetic and copies ran while one was open for 4% of the time, Pallas kernels for 0%

profile of v1, /device:TPU:70, one launch (start us, length us, event | category | flops | bytes accessed | tf_op | source)
XLA Modules:
  0.0 164.4 jit_solution(14843492271181206647)
XLA Ops:
  0.0 1.1 copy.50
  1.1 1.1 copy.51
  2.3 0.0 copy-start
  2.3 0.1 pad_maximum_fusion.1
  2.3 1.0 copy.52
  3.3 7.1 %all-to-all-start.1 = ((bf16[128,8,2,128]{3,0,2,1:T(8,128)(2,1)}), bf16[128,8,2,128]{3,0,2,1:T(8,128)(2,1)S(1)}, u32[]{:S(2)}, u32[]{:S(2)}) async-start(bf16[128,8,2,128]{3,0,2,1:T(8,128)(2,1)} %copy.52), calls=%async_computation.1 | async-start | bytes 1048576 | tf_op jit(solution)/shard_map/all_to_all | solution.py:133
  10.4 0.0 copy-done
  10.4 1.3 copy.47
  11.7 0.0 copy-start.1
  11.7 16.2 %all-to-all-done.1 = bf16[128,8,2,128]{3,0,2,1:T(8,128)(2,1)S(1)} async-done(((bf16[128,8,2,128]{3,0,2,1:T(8,128)(2,1)}), bf16[128,8,2,128]{3,0,2,1:T(8,128)(2,1)S(1)}, u32[]{:S(2)}, u32[]{:S(2)}) %all-to-all-start.1) | async-done | bytes 524320 | tf_op jit(solution)/shard_map/all_to_all | solution.py:133
  27.9 3.6 %all-to-all-start = ((bf16[128,32,128]{0,2,1:T(8,128)(2,1)}), bf16[128,32,128]{0,2,1:T(8,128)(2,1)S(1)}, u32[]{:S(2)}, u32[]{:S(2)}) async-start(bf16[128,32,128]{0,2,1:T(8,128)(2,1)} %bitcast.6), calls=%async_computation | async-start | bytes 2097152 | tf_op jit(solution)/shard_map/all_to_all | solution.py:132
  31.5 0.0 copy-done.1
  31.5 0.1 copy.45
  31.6 0.1 reduce
  31.8 0.2 convert_reduce_fusion.2
  32.0 1.9 %collective-permute-start = (bf16[1024,1,2,128]{3,0,2,1:T(8,128)(2,1)S(1)}, bf16[1024,1,2,128]{3,0,2,1:T(8,128)(2,1)S(1)}, u32[]{:S(2)}, u32[]{:S(2)}) collective-permute-start(bf16[1024,1,2,128]{3,0,2,1:T(8,128)(2,1)S(1)} %bitcast.43), channel_id=1, source_target_pairs={{0,8},{8,16},{16,24},{24,32},{32,40},{40,48},{48,56},{56,64},{64,7... | collective-permute-start | bytes 1572872 | tf_op jit(solution)/shard_map/ppermute | solution.py:25
  34.0 0.6 gather_fusion
  34.7 0.1 copy.46
  34.7 0.6 reshape.192.bounds_ref
  35.4 7.2 %collective-permute-done = bf16[1024,1,2,128]{3,0,2,1:T(8,128)(2,1)S(1)} collective-permute-done((bf16[1024,1,2,128]{3,0,2,1:T(8,128)(2,1)S(1)}, bf16[1024,1,2,128]{3,0,2,1:T(8,128)(2,1)S(1)}, u32[]{:S(2)}, u32[]{:S(2)}) %collective-permute-start) | collective-permute-done | bytes 524320 | tf_op jit(solution)/shard_map/ppermute | solution.py:25
  42.5 2.2 %collective-permute-start.1 = (bf16[1024,1,2,128]{3,0,2,1:T(8,128)(2,1)S(1)}, bf16[1024,1,2,128]{3,0,2,1:T(8,128)(2,1)}, u32[]{:S(2)}, u32[]{:S(2)}) collective-permute-start(bf16[1024,1,2,128]{3,0,2,1:T(8,128)(2,1)S(1)} %collective-permute-done), channel_id=1, source_target_pairs={{0,8},{8,16},{16,24},{24,32},{32,40},{40,48},{48,56},{56,64},{64,7... | collective-permute-start | bytes 1572872 | tf_op jit(solution)/shard_map/ppermute | solution.py:25
  44.7 0.1 convert_reduce_fusion
  44.9 0.1 convert_reduce_fusion.1
  45.0 1.0 copy.54.q_doc_ref
  46.0 0.6 fusion.k_doc_ref
  46.6 14.0 %all-to-all-done = bf16[128,32,128]{0,2,1:T(8,128)(2,1)S(1)} async-done(((bf16[128,32,128]{0,2,1:T(8,128)(2,1)}), bf16[128,32,128]{0,2,1:T(8,128)(2,1)S(1)}, u32[]{:S(2)}, u32[]{:S(2)}) %all-to-all-start) | async-done | bytes 1048608 | tf_op jit(solution)/shard_map/all_to_all | solution.py:132
  60.6 0.7 copy.49
  61.3 1.2 copy.60
  62.5 0.0 collective-permute-done.1
  62.5 1.1 pad_maximum_fusion
  63.6 1.3 slice_bitcast_fusion
  64.9 74.8 %shard_map.46 = bf16[1024,512]{1,0:T(8,128)(2,1)} custom-call(s32[8]{0:T(128)} %reshape.192.bounds_ref, s32[1024,1]{1,0:T(8,128)} %copy.54.q_doc_ref, s32[12,256]{1,0:T(8,128)} %fusion.k_doc_ref, bf16[1024,512]{1,0:T(8,128)(2,1)} %bitcast.37, bf16[3072,128]{1,0:T(8,128)(2,1)} %get-tuple-element.6.k_ref, bf16[3072,128]{1,0:T(8,128)(2,1)} %get-tuple-element.5.v_ref), custom_call_target="tpu_custom_call" | custom-call | tf_op jit(solution)/shard_map/pallas_call | solution.py:99
  139.8 1.3 reshape.196
  141.1 21.3 %all_to_all.48 = bf16[1024,4,128]{2,1,0:T(4,128)(2,1)S(1)} all-to-all(bf16[1024,4,128]{2,1,0:T(4,128)(2,1)S(1)} %reshape.196), channel_id=1, replica_groups=mesh['dp'=2,'blk'=32,'uly'=8] {'uly'}, dimensions={0} | all-to-all | bytes 2097152 | tf_op jit(solution)/shard_map/all_to_all | solution.py:160
  162.5 0.4 copy.61
  162.8 1.6 reshape.197
  (11 shorter events, 0.2 us)
Async XLA Ops:
  2.3 8.2 %copy-start = (bf16[128,4096]{1,0:T(8,128)(2,1)S(1)}, bf16[128,4096]{1,0:T(8,128)(2,1)}, u32[]{:S(2)}) copy-start(bf16[128,4096]{1,0:T(8,128)(2,1)} %param.4) | copy-start | bytes 3145732
  3.3 24.6 %all-to-all-start.1 = ((bf16[128,8,2,128]{3,0,2,1:T(8,128)(2,1)}), bf16[128,8,2,128]{3,0,2,1:T(8,128)(2,1)S(1)}, u32[]{:S(2)}, u32[]{:S(2)}) async-start(bf16[128,8,2,128]{3,0,2,1:T(8,128)(2,1)} %copy.52), calls=%async_computation.1 | async-start | bytes 1048576 | tf_op jit(solution)/shard_map/all_to_all | solution.py:133
  11.7 19.8 %copy-start.1 = (s32[21]{0:T(128)S(1)}, s32[21]{0:T(128)}, u32[]{:S(2)}) copy-start(s32[21]{0:T(128)} %param.7) | copy-start | bytes 256
  27.9 32.7 %all-to-all-start = ((bf16[128,32,128]{0,2,1:T(8,128)(2,1)}), bf16[128,32,128]{0,2,1:T(8,128)(2,1)S(1)}, u32[]{:S(2)}, u32[]{:S(2)}) async-start(bf16[128,32,128]{0,2,1:T(8,128)(2,1)} %bitcast.6), calls=%async_computation | async-start | bytes 2097152 | tf_op jit(solution)/shard_map/all_to_all | solution.py:132
  32.0 10.5 %collective-permute-start = (bf16[1024,1,2,128]{3,0,2,1:T(8,128)(2,1)S(1)}, bf16[1024,1,2,128]{3,0,2,1:T(8,128)(2,1)S(1)}, u32[]{:S(2)}, u32[]{:S(2)}) collective-permute-start(bf16[1024,1,2,128]{3,0,2,1:T(8,128)(2,1)S(1)} %bitcast.43), channel_id=1, source_target_pairs={{0,8},{8,16},{16,24},{24,32},{32,40},{40,48},{48,56},{56,64},{64,7... | collective-permute-start | bytes 1572872 | tf_op jit(solution)/shard_map/ppermute | solution.py:25
  42.5 20.0 %collective-permute-start.1 = (bf16[1024,1,2,128]{3,0,2,1:T(8,128)(2,1)S(1)}, bf16[1024,1,2,128]{3,0,2,1:T(8,128)(2,1)}, u32[]{:S(2)}, u32[]{:S(2)}) collective-permute-start(bf16[1024,1,2,128]{3,0,2,1:T(8,128)(2,1)S(1)} %collective-permute-done), channel_id=1, source_target_pairs={{0,8},{8,16},{16,24},{24,32},{32,40},{40,48},{48,56},{56,64},{64,7... | collective-permute-start | bytes 1572872 | tf_op jit(solution)/shard_map/ppermute | solution.py:25
